TPU v7x, 1024 devices: a whole 4x8x16 slice. The times are simulated.
1024 devices in a mesh: dom: 32 (over z, core), grp: 8 (over y), rep: 4 (over x).
Axes of the slice: x: 4, y: 8, z: 16, core: 2. Of those that a mesh axis runs over, the one named last changes fastest.
Arguments:
- features: bfloat16 [8192, 768], P(('rep', 'grp')), may hold values from -6 to 6
- tiles: bfloat16 [32, 4, 12, 256, 256], P('dom', 'rep', None, 'grp'), may hold values from 0 to 0.039794922
- columns: int32 [2, 32, 4, 8], replicated, may hold values from 0 to 7, as said below
- counts: int32 [2, 32, 4], replicated, may hold values from 1 to 8, as said below
- weights: bfloat16 [2, 768, 768], replicated, may hold values from -0.21875 to 0.21875
Outputs:
- aggregated: bfloat16 [8192, 768], P(('dom', 'grp', 'rep'))
Inputs may be any that keep to these rules, and one draw needn't show every extreme that they name: `columns`: within each list, the entries below the count name distinct source panels of the group; later entries are unused. An owner's two counts in a column group add up to 9 to 15, and 15 is reached; over all owners of a column group they add up to 384.
All inputs are finite; a program needn't handle non-finite values.
Results may differ from a plain program's by a relative error of at most 0.0085.
Values may be sent and summed in bfloat16 or wider, within the bound.
No kernel may reach another device: no remote copies, remote signals or barrier semaphores. Data moves between devices by JAX's collectives and lax.ppermute only.
A program may use at most 32 MiB of HBM per device.

v0:
```python
import jax
import jax.numpy as jnp
from jax import lax
from jax.sharding import PartitionSpec as P


def on_device(features, tiles, columns, counts, weights):
    slot_count = tiles.shape[2]
    strip_rows = tiles.shape[3]
    tile_cols = tiles.shape[4]
    list_len = columns.shape[3]
    feat_dim = features.shape[1]
    chip_count = lax.axis_size("z")
    core_count = lax.axis_size("core")
    owners_count = chip_count * core_count
    my_core = lax.axis_index("core")
    me = lax.axis_index("z") * core_count + my_core
    column_group = lax.axis_index("rep")
    max_load = 2 * list_len

    swap = [(0, 1), (1, 0)]
    half = feat_dim // core_count
    mine = lax.dynamic_slice_in_dim(features, my_core * half, half, axis=1)
    panels = lax.all_gather(mine, "grp", axis=0, tiled=True)

    first_counts = counts[0][:, column_group]
    group_loads = first_counts + counts[1][:, column_group]
    owner_starts = jnp.cumsum(group_loads) - group_loads

    strips = tiles.reshape(slot_count, strip_rows, tile_cols)
    chip_loads = group_loads.reshape(chip_count, core_count).sum(axis=1)
    chip_starts = owner_starts.reshape(chip_count, core_count)[:, 0]
    chip_slot = (chip_starts - me + owners_count - 1) // owners_count
    chip_slot = jnp.clip(chip_slot, 0, slot_count - 1)
    chip_place = me + chip_slot * owners_count
    chip_has = (chip_place >= chip_starts) & (chip_place < chip_starts + chip_loads)
    outgoing = jnp.where(chip_has[:, None, None], jnp.take(strips, chip_slot, axis=0), jnp.zeros((), strips.dtype))
    from_chips = lax.all_to_all(outgoing, "z", split_axis=0, concat_axis=0, tiled=True)
    from_sibling = lax.ppermute(from_chips, "core", swap)
    from_core0 = jnp.where(my_core == 0, from_chips, from_sibling)
    from_core1 = jnp.where(my_core == 0, from_sibling, from_chips)
    incoming = jnp.stack([from_core0, from_core1], axis=1).reshape(owners_count, strip_rows, tile_cols)

    chip_first = me - my_core
    owner_ids = chip_first + jnp.arange(core_count, dtype=jnp.int32)
    entry = jnp.arange(max_load, dtype=jnp.int32)[None, :]
    starts = owner_starts[owner_ids][:, None]
    loads = group_loads[owner_ids][:, None]
    firsts = first_counts[owner_ids][:, None]
    entry_valid = entry < loads
    entry_worker = (starts + entry) % owners_count
    entry_rel = (entry >= firsts).astype(jnp.int32)
    entry_k = jnp.clip(entry - entry_rel * firsts, 0, list_len - 1)
    pair_columns = columns[:, owner_ids, column_group, :]
    entry_col = pair_columns[entry_rel, jnp.arange(core_count)[:, None], entry_k]
    entry_valid = entry_valid.reshape(-1)
    entry_rel = entry_rel.reshape(-1)
    entry_col = entry_col.reshape(-1)
    blocks = jnp.take(incoming, entry_worker.reshape(-1), axis=0)
    blocks = jnp.where(entry_valid[:, None, None], blocks, jnp.zeros((), blocks.dtype))
    n_entries = core_count * max_load
    rows = n_entries * strip_rows
    row_col = jnp.repeat(entry_col, strip_rows)
    lane_panel = jnp.arange(list_len * tile_cols, dtype=jnp.int32) // tile_cols
    placed = jnp.tile(blocks.reshape(rows, tile_cols), (1, list_len))
    placed = jnp.where(row_col[:, None] == lane_panel[None, :], placed, jnp.zeros((), placed.dtype))
    products = jnp.dot(placed, panels, preferred_element_type=jnp.float32).astype(jnp.bfloat16)
    row_rel = jnp.repeat(entry_rel, strip_rows)[:, None]
    zero = jnp.zeros((), products.dtype)
    my_weights = lax.dynamic_slice_in_dim(weights, my_core * half, half, axis=1)
    terms = jnp.dot(jnp.where(row_rel == 0, products, zero), my_weights[0], preferred_element_type=jnp.float32)
    terms = terms + jnp.dot(jnp.where(row_rel == 1, products, zero), my_weights[1], preferred_element_type=jnp.float32)
    partial_value = jnp.sum(terms.reshape(core_count, max_load, strip_rows, feat_dim), axis=1)
    rep_count = lax.axis_size("rep")
    pieces = partial_value.reshape(core_count * rep_count, strip_rows // rep_count, feat_dim)
    pieces = lax.all_to_all(pieces, ("core", "rep"), split_axis=0, concat_axis=0, tiled=True)
    return jnp.sum(pieces, axis=0).astype(jnp.bfloat16)


def solution(mesh):
    dom_size, grp_size, rep_size = mesh.devices.shape
    split = jax.sharding.Mesh(
        mesh.devices.reshape(dom_size // 2, 2, grp_size, rep_size), ("z", "core", "grp", "rep")
    )
    return jax.shard_map(
        on_device,
        mesh=split,
        in_specs=(P(("rep", "grp"), None), P(("z", "core"), "rep", None, "grp", None), P(), P(), P()),
        out_specs=P(("z", "core", "grp", "rep"), None),
        check_vma=False,
    )
```

profile of v0, /device:TPU:1, one launch (start us, length us, event | category | flops | bytes accessed | tf_op | source)
XLA Modules:
  0.0 95.0 jit_solution(1529621452061249977)
XLA Ops:
  6.5 1.8 %constant_dynamic-slice_fusion = bf16[256,384]{1,0:T(8,128)(2,1)} fusion(bf16[256,768]{1,0:T(8,128)(2,1)} %param.5, s32[]{:T(128)S(6)} %select_n.173), kind=kLoop, calls=%fused_computation.69 | loop fusion | bytes 393220 | tf_op jit(solution)/shard_map/dynamic_slice | solution.py:23
  8.4 0.7 fusion.43
  9.1 0.5 broadcast.527
  9.6 0.7 fusion.41
  11.2 1.5 %gather_fusion.5 = bf16[16,32,256]{2,1,0:T(8,128)(2,1)S(1)} fusion(bf16[12,32,256]{2,1,0:T(8,128)(2,1)} %bitcast.46, s32[1024]{0:T(1024)S(1)} %pad_clamp_fusion.1), kind=kCustom, calls=%fused_computation.5 | custom fusion | bytes 524352 | tf_op jit(solution)/shard_map/jit(_take)/gather | solution.py:37
  12.7 0.8 select_select_fusion
  13.5 19.4 %all-to-all-start = ((bf16[16,32,256]{2,1,0:T(8,128)(2,1)}), bf16[16,32,256]{2,1,0:T(8,128)(2,1)S(1)}, u32[]{:S(2)}, u32[]{:S(2)}) async-start(bf16[16,32,256]{2,1,0:T(8,128)(2,1)} %select_select_fusion), calls=%async_computation | async-start | bytes 524288 | tf_op jit(solution)/shard_map/all_to_all | solution.py:38
  33.0 0.6 gather_fusion.4
  33.9 0.6 gather_fusion.3
  34.5 0.6 gather_fusion
  35.3 11.4 %all-to-all-done = bf16[16,32,256]{2,1,0:T(8,128)(2,1)S(1)} async-done(((bf16[16,32,256]{2,1,0:T(8,128)(2,1)}), bf16[16,32,256]{2,1,0:T(8,128)(2,1)S(1)}, u32[]{:S(2)}, u32[]{:S(2)}) %all-to-all-start) | async-done | bytes 262176 | tf_op jit(solution)/shard_map/all_to_all | solution.py:38
  46.7 7.5 %collective-permute-start = (bf16[16,32,256]{2,1,0:T(8,128)(2,1)S(1)}, bf16[16,32,256]{2,1,0:T(8,128)(2,1)S(1)}, u32[]{:S(2)}, u32[]{:S(2)}) collective-permute-start(bf16[16,32,256]{2,1,0:T(8,128)(2,1)S(1)} %all-to-all-done), channel_id=1, source_target_pairs={{0,32},{32,0},{1,33},{33,1},{2,34},{34,2},{3,35},{35,3},{4,36},{36... | collective-permute-start | bytes 786440 | tf_op jit(solution)/shard_map/ppermute | solution.py:39
  54.9 0.6 gather_fusion.1
  55.5 0.8 gather_fusion.2
  57.0 0.6 gather_fusion.6
  57.6 0.3 fusion.10
  58.0 0.6 tile.8
  58.5 3.4 %copy.17 = bf16[128,8,8,256]{3,1,2,0:T(8,128)(2,1)} copy(bf16[128,8,8,256]{3,2,1,0:T(8,128)(2,1)S(1)} %bitcast.41) | data formatting | bytes 8388608
  61.9 5.0 %fusion.4 = bf16[1024,384]{1,0:T(8,128)(2,1)S(1)} fusion(bf16[2048,384]{1,0:T(8,128)(2,1)} %all-gather.2.cloned.1.call-done, bf16[1024,2048]{1,0:T(8,128)(2,1)} %bitcast.43, s32[2048]{0:T(1024)S(1)} %add_select_fusion.1, s32[1024]{0:T(1024)S(1)} %eq.61), kind=kOutput, calls=%fused_computation.13 | convolution fusion | flops 1615200256 | bytes 6565888 | tf_op jit(solution)/shard_map/dot_general | solution.py:67
  67.0 1.0 %fusion.6 = f32[1024,768]{1,0:T(8,128)S(1)} fusion(bf16[1024,384]{1,0:T(8,128)(2,1)S(1)} %fusion.4, pred[1024]{0:T(1024)(128)(4,1)S(1)} %eq.60, bf16[2,768,768]{2,1,0:T(8,128)(2,1)S(1)} %copy-done, s32[]{:T(128)S(6)} %select_n.173), kind=kOutput, calls=%fused_computation.15 | convolution fusion | flops 604372992 | bytes 4523012 | tf_op jit(solution)/shard_map/dot_general | solution.py:71
  68.0 2.7 %convolution_add_fusion = f32[1024,768]{1,0:T(8,128)} fusion(f32[1024,768]{1,0:T(8,128)S(1)} %fusion.6, bf16[1024,384]{1,0:T(8,128)(2,1)S(1)} %fusion.4, pred[1024]{0:T(1024)(128)(4,1)S(1)} %eq.69, bf16[2,768,768]{2,1,0:T(8,128)(2,1)S(1)} %copy-done, s32[]{:T(128)S(6)} %add.243, s32[]{:T(128)S(6)} %select_n.173), kind=kOutput, calls=%fused_computation.12 | convolution fusion | flops 605159424 | bytes 7668744 | tf_op jit(solution)/shard_map/dot_general | solution.py:72
  70.8 2.1 %reduce_sum.28 = f32[2,32,768]{2,1,0:T(8,128)S(1)} reduce(f32[2,16,32,768]{3,2,1,0:T(8,128)} %bitcast.42, f32[]{:T(128)} %constant.124.clone.1), dimensions={1}, to_apply=%region_2.3 | reduce | flops 737280 | bytes 3342340 | tf_op jit(solution)/shard_map/reduce_sum | solution.py:73
  72.8 14.7 %all_to_all.10 = f32[8,8,768]{2,1,0:T(8,128)S(1)} all-to-all(f32[8,8,768]{2,1,0:T(8,128)S(1)} %bitcast.45), channel_id=1, replica_groups=mesh['z'=16,'core'=2,'grp'=8,'rep'=4] {'core','rep'}, dimensions={0} | all-to-all | bytes 393216 | tf_op jit(solution)/shard_map/all_to_all | solution.py:76
  87.5 0.6 reduce_sum.29
  (49 shorter events, 2.9 us)
Async XLA Ops:
  6.5 60.4 %copy-start = (bf16[2,768,768]{2,1,0:T(8,128)(2,1)S(1)}, bf16[2,768,768]{2,1,0:T(8,128)(2,1)}, u32[]{:S(2)}) copy-start(bf16[2,768,768]{2,1,0:T(8,128)(2,1)} %param.9) | copy-start | bytes 7077892
  6.5 48.2 %copy-start.1 = (s32[2,32,4,8]{1,3,2,0:T(8,128)S(1)}, s32[2,32,4,8]{1,3,2,0:T(8,128)}, u32[]{:S(2)}) copy-start(s32[2,32,4,8]{1,3,2,0:T(8,128)} %param.7) | copy-start | bytes 24580
  6.5 55.4 %all-gather.2.cloned.1.call-start = ((), (), s32[]{:S(2)}) async-start(), calls=%async_computation.2 | async-start | bytes 1769472 | tf_op jit(solution)/shard_map/all_gather | solution.py:24
  13.5 33.2 %all-to-all-start = ((bf16[16,32,256]{2,1,0:T(8,128)(2,1)}), bf16[16,32,256]{2,1,0:T(8,128)(2,1)S(1)}, u32[]{:S(2)}, u32[]{:S(2)}) async-start(bf16[16,32,256]{2,1,0:T(8,128)(2,1)} %select_select_fusion), calls=%async_computation | async-start | bytes 524288 | tf_op jit(solution)/shard_map/all_to_all | solution.py:38
  46.7 10.2 %collective-permute-start = (bf16[16,32,256]{2,1,0:T(8,128)(2,1)S(1)}, bf16[16,32,256]{2,1,0:T(8,128)(2,1)S(1)}, u32[]{:S(2)}, u32[]{:S(2)}) collective-permute-start(bf16[16,32,256]{2,1,0:T(8,128)(2,1)S(1)} %all-to-all-done), channel_id=1, source_target_pairs={{0,32},{32,0},{1,33},{33,1},{2,34},{34,2},{3,35},{35,3},{4,36},{36... | collective-permute-start | bytes 786440 | tf_op jit(solution)/shard_map/ppermute | solution.py:39
Sparse Core Ops, SparseCore 0:
  10.0 51.8 all-gather.1
where the time goes:
time: 95.3 us; the launch traced here: 95 us
  starting transfers between devices  26.9 us (28%)
  blocking collectives  14.7 us (15%)
  local copies, waits for them, and re-layouts  14 us (15%)
  between operations  13.6 us (14%)
  waiting for transfers between devices  11.4 us (12%)
  matrix products  8.81 us (9%)
  other arithmetic  5.62 us (6%)
    all_to_all x1, starting transfers between devices, on_device(): lax.all_to_all(outgoing, 'z', split_axis=0, concat_axis=0, tiled=True)  19.4 us
    all_to_all x1, blocking collectives, on_device(): lax.all_to_all(pieces, ('core', 'rep'), split_axis=0, concat_axis=0, tile...  14.7 us
    all_to_all x1, waiting for transfers between devices, on_device(): lax.all_to_all(outgoing, 'z', split_axis=0, concat_axis=0, tiled=True)  11.4 us
    ppermute x1, starting transfers between devices, on_device(): from_sibling = lax.ppermute(from_chips, 'core', swap)  7.46 us
    dot_general x1, matrix products, on_device(): jnp.dot(placed, panels, preferred_element_type=jnp.float32)  5.05 us
    unnamed x6, local copies, waits for them, and re-layouts  3.54 us
    dot_general x1, matrix products, on_device(): jnp.dot(jnp.where(row_rel == 1, products, zero), my_weights[1], preferred...  2.73 us
    reduce_sum x1, other arithmetic, on_device(): jnp.sum(terms.reshape(core_count, max_load, strip_rows, feat_dim), axis=1)  2.06 us
  transfers between devices with their start and end apart: 3, of which 1 were waited for; matrix products, arithmetic and copies ran while one was open for 16% of the time, Pallas kernels for 0%

commit v1 on v0

--- a/solution.py
+++ b/solution.py
@@ -43,34 +43,38 @@
 
     chip_first = me - my_core
     owner_ids = chip_first + jnp.arange(core_count, dtype=jnp.int32)
-    entry = jnp.arange(max_load, dtype=jnp.int32)[None, :]
-    starts = owner_starts[owner_ids][:, None]
-    loads = group_loads[owner_ids][:, None]
-    firsts = first_counts[owner_ids][:, None]
-    entry_valid = entry < loads
-    entry_worker = (starts + entry) % owners_count
-    entry_rel = (entry >= firsts).astype(jnp.int32)
-    entry_k = jnp.clip(entry - entry_rel * firsts, 0, list_len - 1)
+    starts = owner_starts[owner_ids]
+    firsts = first_counts[owner_ids]
     pair_columns = columns[:, owner_ids, column_group, :]
-    entry_col = pair_columns[entry_rel, jnp.arange(core_count)[:, None], entry_k]
-    entry_valid = entry_valid.reshape(-1)
-    entry_rel = entry_rel.reshape(-1)
-    entry_col = entry_col.reshape(-1)
-    blocks = jnp.take(incoming, entry_worker.reshape(-1), axis=0)
-    blocks = jnp.where(entry_valid[:, None, None], blocks, jnp.zeros((), blocks.dtype))
-    n_entries = core_count * max_load
-    rows = n_entries * strip_rows
-    row_col = jnp.repeat(entry_col, strip_rows)
-    lane_panel = jnp.arange(list_len * tile_cols, dtype=jnp.int32) // tile_cols
-    placed = jnp.tile(blocks.reshape(rows, tile_cols), (1, list_len))
-    placed = jnp.where(row_col[:, None] == lane_panel[None, :], placed, jnp.zeros((), placed.dtype))
-    products = jnp.dot(placed, panels, preferred_element_type=jnp.float32).astype(jnp.bfloat16)
-    row_rel = jnp.repeat(entry_rel, strip_rows)[:, None]
-    zero = jnp.zeros((), products.dtype)
+    pair_counts = counts[:, owner_ids, column_group]
+    kk = jnp.arange(list_len, dtype=jnp.int32)
+    panel_ids = jnp.arange(list_len, dtype=jnp.int32)
+    hit = (pair_columns[None, :, :, :] == panel_ids[:, None, None, None]) & (
+        kk[None, None, None, :] < pair_counts[None, :, :, None]
+    )
+    slot_valid = jnp.any(hit, axis=3)
+    slot_k = jnp.sum(jnp.where(hit, kk[None, None, None, :], 0), axis=3)
+    relation = jnp.arange(2, dtype=jnp.int32)
+    slot_place = starts[None, None, :] + relation[None, :, None] * firsts[None, None, :] + slot_k
+    slot_worker = jnp.transpose(slot_place % owners_count, (0, 2, 1)).reshape(-1)
+    slot_valid = jnp.transpose(slot_valid, (0, 2, 1)).reshape(-1)
+    blocks = jnp.take(incoming, slot_worker, axis=0)
+    blocks = jnp.where(slot_valid[:, None, None], blocks, jnp.zeros((), blocks.dtype))
+    per_panel = core_count * 2 * strip_rows
+    blocks = blocks.reshape(list_len, per_panel, tile_cols)
+    products = jnp.einsum(
+        "jmt,jtf->jmf", blocks, panels.reshape(list_len, tile_cols, half), preferred_element_type=jnp.float32
+    ).astype(jnp.bfloat16)
+    sums = jnp.sum(products.astype(jnp.float32), axis=0).reshape(core_count, 2, strip_rows, half)
     my_weights = lax.dynamic_slice_in_dim(weights, my_core * half, half, axis=1)
-    terms = jnp.dot(jnp.where(row_rel == 0, products, zero), my_weights[0], preferred_element_type=jnp.float32)
-    terms = terms + jnp.dot(jnp.where(row_rel == 1, products, zero), my_weights[1], preferred_element_type=jnp.float32)
-    partial_value = jnp.sum(terms.reshape(core_count, max_load, strip_rows, feat_dim), axis=1)
+    partial_value = None
+    for q in range(2):
+        lhs = sums[:, q].reshape(core_count * strip_rows, half)
+        top = lhs.astype(jnp.bfloat16)
+        rest = (lhs - top.astype(jnp.float32)).astype(jnp.bfloat16)
+        part = jnp.dot(top, my_weights[q], preferred_element_type=jnp.float32)
+        part = part + jnp.dot(rest, my_weights[q], preferred_element_type=jnp.float32)
+        partial_value = part if partial_value is None else partial_value + part
     rep_count = lax.axis_size("rep")
     pieces = partial_value.reshape(core_count * rep_count, strip_rows // rep_count, feat_dim)
     pieces = lax.all_to_all(pieces, ("core", "rep"), split_axis=0, concat_axis=0, tiled=True)

time: 95.3 us -> 87.4 us (0.917)
  matrix products: 8.81 us -> 2.77 us
  local copies, waits for them, and re-layouts: 14 us -> 8.86 us
  waiting for transfers between devices: 11.4 us -> 16.3 us
  other arithmetic: 5.62 us -> 3.74 us
    dot_general x3 -> x5, matrix products: 8.81 us -> 2.77 us  [the longest x1 1.86 us: on_device(): jnp.einsum('jmt,jtf->jmf', blocks, panels.reshape(list_len, tile_cols, ha...]
    all_gather x1, waiting for transfers between devices: 0.01 us -> 5.55 us  [on_device(): panels = lax.all_gather(mine, 'grp', axis=0, tiled=True)]
    unnamed x6 -> x8, local copies, waits for them, and re-layouts: 3.54 us -> 0.26 us
    reduce_sum x1, other arithmetic: 2.06 us -> 0.15 us  [on_device(): slot_k = jnp.sum(jnp.where(hit, kk[None, None, None, :], 0), axis=3)]
    all_to_all x1, waiting for transfers between devices: 11.4 us -> 9.66 us  [on_device(): lax.all_to_all(outgoing, 'z', split_axis=0, concat_axis=0, tiled=True)]
    ppermute x1, waiting for transfers between devices: 0.01 us -> 1.11 us  [on_device(): from_sibling = lax.ppermute(from_chips, 'core', swap)]
  transfers between devices with their start and end apart: 3 -> 3, of which waited for: 1 -> 3; matrix products, arithmetic and copies ran while one was open for 16% -> 12% of each run, Pallas kernels for 0% -> 0%
where the time goes in v1:
time: 87.4 us; the launch traced here: 87 us
  starting transfers between devices  26.9 us (31%)
  waiting for transfers between devices  16.3 us (19%)
  blocking collectives  14.8 us (17%)
  between operations  13.6 us (16%)
  local copies, waits for them, and re-layouts  8.86 us (10%)
  other arithmetic  3.74 us (4%)
  matrix products  2.77 us (3%)
    all_to_all x1, starting transfers between devices, on_device(): lax.all_to_all(outgoing, 'z', split_axis=0, concat_axis=0, tiled=True)  19.4 us
    all_to_all x1, blocking collectives, on_device(): lax.all_to_all(pieces, ('core', 'rep'), split_axis=0, concat_axis=0, tile...  14.8 us
    all_to_all x1, waiting for transfers between devices, on_device(): lax.all_to_all(outgoing, 'z', split_axis=0, concat_axis=0, tiled=True)  9.66 us
    ppermute x1, starting transfers between devices, on_device(): from_sibling = lax.ppermute(from_chips, 'core', swap)  7.46 us
    all_gather x1, waiting for transfers between devices, on_device(): panels = lax.all_gather(mine, 'grp', axis=0, tiled=True)  5.55 us
    dot_general x1, matrix products, on_device(): jnp.einsum('jmt,jtf->jmf', blocks, panels.reshape(list_len, tile_cols, ha...  1.86 us
    dynamic_slice x1, local copies, waits for them, and re-layouts, on_device(): mine = lax.dynamic_slice_in_dim(features, my_core * half, half, axis=1)  1.78 us
  transfers between devices with their start and end apart: 3, of which 3 were waited for; matrix products, arithmetic and copies ran while one was open for 12% of the time, Pallas kernels for 0%

profile of v1, /device:TPU:1, one launch (start us, length us, event | category | flops | bytes accessed | tf_op | source)
XLA Modules:
  0.0 87.0 jit_solution(9327911866936671132)
XLA Ops:
  6.6 1.8 %constant_dynamic-slice_fusion = bf16[256,384]{1,0:T(8,128)(2,1)} fusion(bf16[256,768]{1,0:T(8,128)(2,1)} %param.5, s32[]{:T(128)S(6)} %select_n.117), kind=kLoop, calls=%fused_computation.61 | loop fusion | bytes 393220 | tf_op jit(solution)/shard_map/dynamic_slice | solution.py:23
  8.4 0.7 fusion.24
  9.1 0.5 broadcast.316
  9.6 0.7 fusion.22
  11.2 1.5 %gather_fusion.4 = bf16[16,32,256]{2,1,0:T(8,128)(2,1)S(1)} fusion(bf16[12,32,256]{2,1,0:T(8,128)(2,1)} %bitcast.64, s32[1024]{0:T(1024)S(1)} %pad_clamp_fusion.1), kind=kCustom, calls=%fused_computation.4 | custom fusion | bytes 524352 | tf_op jit(solution)/shard_map/jit(_take)/gather | solution.py:37
  12.7 0.8 select_select_fusion
  13.5 19.4 %all-to-all-start = ((bf16[16,32,256]{2,1,0:T(8,128)(2,1)}), bf16[16,32,256]{2,1,0:T(8,128)(2,1)S(1)}, u32[]{:S(2)}, u32[]{:S(2)}) async-start(bf16[16,32,256]{2,1,0:T(8,128)(2,1)} %select_select_fusion), calls=%async_computation | async-start | bytes 524288 | tf_op jit(solution)/shard_map/all_to_all | solution.py:38
  33.1 0.6 gather_fusion.1
  33.9 0.6 gather_fusion.2
  34.5 0.6 gather_fusion.3
  35.3 0.6 gather_fusion
  37.0 9.7 %all-to-all-done = bf16[16,32,256]{2,1,0:T(8,128)(2,1)S(1)} async-done(((bf16[16,32,256]{2,1,0:T(8,128)(2,1)}), bf16[16,32,256]{2,1,0:T(8,128)(2,1)S(1)}, u32[]{:S(2)}, u32[]{:S(2)}) %all-to-all-start) | async-done | bytes 262176 | tf_op jit(solution)/shard_map/all_to_all | solution.py:38
  46.7 7.5 %collective-permute-start = (bf16[16,32,256]{2,1,0:T(8,128)(2,1)S(1)}, bf16[16,32,256]{2,1,0:T(8,128)(2,1)S(1)}, u32[]{:S(2)}, u32[]{:S(2)}) collective-permute-start(bf16[16,32,256]{2,1,0:T(8,128)(2,1)S(1)} %all-to-all-done), channel_id=1, source_target_pairs={{0,32},{32,0},{1,33},{33,1},{2,34},{34,2},{3,35},{35,3},{4,36},{36... | collective-permute-start | bytes 786440 | tf_op jit(solution)/shard_map/ppermute | solution.py:39
  54.2 1.1 %collective-permute-done = bf16[16,32,256]{2,1,0:T(8,128)(2,1)S(1)} collective-permute-done((bf16[16,32,256]{2,1,0:T(8,128)(2,1)S(1)}, bf16[16,32,256]{2,1,0:T(8,128)(2,1)S(1)}, u32[]{:S(2)}, u32[]{:S(2)}) %collective-permute-start) | collective-permute-done | bytes 262176 | tf_op jit(solution)/shard_map/ppermute | solution.py:39
  55.4 0.6 gather_fusion.5
  56.0 0.3 fusion.2
  56.4 5.5 %all-gather.2.cloned.1.call-done = bf16[2048,384]{1,0:T(8,128)(2,1)} async-done(((bf16[256,384]{1,0:T(8,128)(2,1)}), bf16[2048,384]{1,0:T(8,128)(2,1)}) %all-gather.2.cloned.1.call-update) | async-done | bytes 1572880 | tf_op jit(solution)/shard_map/all_gather | solution.py:24
  61.9 1.9 %convert_reduce_fusion = f32[128,384]{1,0:T(8,128)S(1)} fusion(bf16[8,128,256]{2,1,0:T(8,128)(2,1)S(1)} %fusion.2, bf16[8,256,384]{2,1,0:T(8,128)(2,1)} %bitcast.62), kind=kOutput, calls=%fused_computation.6 | convolution fusion | flops 202457088 | bytes 2293760 | tf_op jit(solution)/shard_map/jmt,jtf->jmf/dot_general | solution.py:65
  63.8 0.2 fusion.3
  64.0 0.2 convolution_add_fusion.1
  64.3 0.2 fusion.4
  64.5 0.2 fusion.1
  64.7 14.8 %all_to_all.10 = f32[8,8,768]{2,1,0:T(8,128)S(1)} all-to-all(f32[8,8,768]{2,1,0:T(8,128)S(1)} %fusion.1), channel_id=1, replica_groups=mesh['z'=16,'core'=2,'grp'=8,'rep'=4] {'core','rep'}, dimensions={0} | all-to-all | bytes 393216 | tf_op jit(solution)/shard_map/all_to_all | solution.py:80
  79.6 0.6 reduce_sum.42
  (48 shorter events, 2.7 us)
Async XLA Ops:
  6.5 57.3 %copy-start = (bf16[2,768,768]{2,1,0:T(8,128)(2,1)S(1)}, bf16[2,768,768]{2,1,0:T(8,128)(2,1)}, u32[]{:S(2)}) copy-start(bf16[2,768,768]{2,1,0:T(8,128)(2,1)} %param.9) | copy-start | bytes 7077892
  6.5 26.4 %copy-start.2 = (s32[2,32,4]{1,2,0:T(4,128)S(1)}, s32[2,32,4]{1,2,0:T(4,128)}, u32[]{:S(2)}) copy-start(s32[2,32,4]{1,2,0:T(4,128)} %param.8) | copy-start | bytes 3076
  6.5 28.6 %copy-start.1 = (s32[2,32,4,8]{1,3,2,0:T(8,128)S(1)}, s32[2,32,4,8]{1,3,2,0:T(8,128)}, u32[]{:S(2)}) copy-start(s32[2,32,4,8]{1,3,2,0:T(8,128)} %param.7) | copy-start | bytes 24580
  6.5 55.4 %all-gather.2.cloned.1.call-start = ((), (), s32[]{:S(2)}) async-start(), calls=%async_computation.2 | async-start | bytes 1769472 | tf_op jit(solution)/shard_map/all_gather | solution.py:24
  13.5 33.2 %all-to-all-start = ((bf16[16,32,256]{2,1,0:T(8,128)(2,1)}), bf16[16,32,256]{2,1,0:T(8,128)(2,1)S(1)}, u32[]{:S(2)}, u32[]{:S(2)}) async-start(bf16[16,32,256]{2,1,0:T(8,128)(2,1)} %select_select_fusion), calls=%async_computation | async-start | bytes 524288 | tf_op jit(solution)/shard_map/all_to_all | solution.py:38
  46.7 8.6 %collective-permute-start = (bf16[16,32,256]{2,1,0:T(8,128)(2,1)S(1)}, bf16[16,32,256]{2,1,0:T(8,128)(2,1)S(1)}, u32[]{:S(2)}, u32[]{:S(2)}) collective-permute-start(bf16[16,32,256]{2,1,0:T(8,128)(2,1)S(1)} %all-to-all-done), channel_id=1, source_target_pairs={{0,32},{32,0},{1,33},{33,1},{2,34},{34,2},{3,35},{35,3},{4,36},{36... | collective-permute-start | bytes 786440 | tf_op jit(solution)/shard_map/ppermute | solution.py:39
Sparse Core Ops, SparseCore 0:
  10.0 51.8 all-gather.1
